TPU v7x, 128 devices: a whole 4x4x4 slice. The times are simulated.
128 devices in a mesh: wide: 32 (over y, x, z_lo), narrow: 4 (over z_hi, core).
Axes of the slice: x: 4, y: 4, z: 4 (z_hi: 2, z_lo: 2; z = z_hi * 2 + z_lo), core: 2. Of those that a mesh axis runs over, the one named last changes fastest.
Arguments:
- sources: int32 [256, 256, 256], P('wide', 'narrow'), may hold values from 0 to 1
- labels: int32 [256, 256, 256], P('wide', 'narrow'), may hold values from 0 to 1, as said below
Outputs:
- distance: float32 [256, 256, 256], P('wide', 'narrow')
Inputs may be any that keep to these rules, and one draw needn't show every extreme that they name: labels marks the union of several periodic balls of radii between 16 and 42 cells; sources marks exactly the labelled cells that have an unlabelled neighbour along one of the six grid directions.
All inputs are finite; a program needn't handle non-finite values.
Results may differ from a plain program's by a relative error of at most 0.00022.
Values sent between devices are 32-bit elements; how exact they have to be, the bound alone decides.
No kernel may reach another device: no remote copies, remote signals or barrier semaphores. Data moves between devices by JAX's collectives and lax.ppermute only.
A program may use at most 128 MiB of HBM per device.

v0:
```python
import math

import jax
import jax.numpy as jnp
from jax import lax
from jax.sharding import PartitionSpec as P

matmul_precision = lax.Precision.HIGH
ALL = ("wide", "narrow")


def cas_table(length):
    positions = jnp.arange(length, dtype=jnp.int32)
    phase_steps = positions[:, None] * positions[None, :] % length
    angles = phase_steps.astype(jnp.float32) * (2.0 * math.pi / length)
    return jnp.cos(angles) + jnp.sin(angles)


def cas_columns(length, positions):
    wavenumbers = jnp.arange(length, dtype=jnp.int32).reshape((length,) + (1,) * positions.ndim)
    phase_steps = wavenumbers * positions[None] % length
    angles = phase_steps.astype(jnp.float32) * (2.0 * math.pi / length)
    return jnp.cos(angles) + jnp.sin(angles)


def window_positions(length, count, width):
    blocks = length // count
    starts = jnp.arange(blocks, dtype=jnp.int32)[:, None] * count - width
    return (starts + jnp.arange(count + 2 * width, dtype=jnp.int32)[None, :]) % length


def eigen(wavenumber, length):
    angles = wavenumber.astype(jnp.float32) * (2.0 * math.pi / length)
    return 2.0 - 2.0 * jnp.cos(angles)


def exchange(blocks):
    shape = blocks.shape
    size = math.prod(shape[1:])
    if size % 1024 == 0:
        blocks = blocks.reshape(shape[0], size // 128, 128)
    return lax.all_to_all(blocks, ALL, 0, 0).reshape(shape)


def to_planes(pencil, cas):
    count_x, count_y, length = pencil.shape
    wide = lax.axis_size("wide")
    narrow = lax.axis_size("narrow")
    span = length // (wide * narrow)
    along_z = jnp.einsum("xyz,zk->kxy", pencil, cas, precision=matmul_precision)
    arrived = exchange(along_z.reshape(wide * narrow, span, count_x, count_y))
    arrived = arrived.reshape(wide, narrow, span, count_x, count_y)
    along_y = jnp.einsum(
        "wqkxy,qyl->kwxl", arrived, cas.reshape(narrow, count_y, length), precision=matmul_precision
    )
    return along_y.reshape(span, wide * count_x, length)


def to_pencil(planes, cas, count_x, count_y):
    span, _, _ = planes.shape
    wide = lax.axis_size("wide")
    narrow = lax.axis_size("narrow")
    send = planes.reshape(span, wide, count_x, narrow, count_y).transpose(1, 3, 0, 2, 4)
    arrived = exchange(send.reshape(wide * narrow, span, count_x, count_y))
    spectrum = arrived.reshape(wide * narrow * span, count_x, count_y)
    return jnp.einsum("kxy,kz->xyz", spectrum, cas, precision=matmul_precision)


def to_pencil_with_halo(spectrum, cas, cas_x, cas_y):
    span, length, _ = spectrum.shape
    _, wide, padded_x = cas_x.shape
    _, narrow, padded_y = cas_y.shape
    along_x = jnp.einsum("kml,mwi->kwil", spectrum, cas_x, precision=matmul_precision)
    windows = jnp.einsum("kwil,lqj->wqkij", along_x, cas_y, precision=matmul_precision)
    send = windows.reshape(wide * narrow, span * padded_x * padded_y)
    arrived = lax.all_to_all(send, ALL, 0, 0)
    spectrum_z = arrived.reshape(wide * narrow * span, padded_x * padded_y)
    values = jnp.einsum("kr,kz->rz", spectrum_z, cas, precision=matmul_precision)
    return values.reshape(padded_x, padded_y, length)


def planes_forward(along_y, cas):
    return jnp.einsum("kxl,xm->kml", along_y, cas, precision=matmul_precision)


def planes_inverse(spectrum, cas):
    along_x = jnp.einsum("kml,mx->kxl", spectrum, cas, precision=matmul_precision)
    return jnp.einsum("kxl,ly->kxy", along_x, cas, precision=matmul_precision)


def central_z(values):
    return 0.5 * (jnp.roll(values, -1, 2) - jnp.roll(values, 1, 2))


def divergence_of_flow(heat, grad_floor):
    inner = heat[1:-1, 1:-1]
    grad_x = 0.5 * (heat[2:, 1:-1] - heat[:-2, 1:-1])
    grad_y = 0.5 * (heat[1:-1, 2:] - heat[1:-1, :-2])
    grad_z = central_z(inner)
    magnitude = jnp.sqrt(grad_x * grad_x + grad_y * grad_y + grad_z * grad_z)
    limited = jnp.maximum(magnitude, grad_floor)
    flow_x = -grad_x / limited
    flow_y = -grad_y / limited
    flow_z = -grad_z / limited
    div_x = 0.5 * (flow_x[2:, 1:-1] - flow_x[:-2, 1:-1])
    div_y = 0.5 * (flow_y[1:-1, 2:] - flow_y[1:-1, :-2])
    div_z = central_z(flow_z[1:-1, 1:-1])
    return div_x + div_y + div_z


def per_device(sources, labels):
    count_x, count_y, length = sources.shape
    span = length // lax.axis_size(ALL)
    heat_time = (length / 8.0) ** 2
    grad_floor = 0.04 / heat_time
    scale = 1.0 / float(length) ** 3
    cas = cas_table(length)
    wave = jnp.arange(length, dtype=jnp.int32)
    wave_z = lax.axis_index(ALL) * span + jnp.arange(span, dtype=jnp.int32)
    laplace = (
        eigen(wave, length)[None, :, None] + eigen(wave, length)[None, None, :]
    ) + eigen(wave_z, length)[:, None, None]
    anchor = (wave_z[:, None, None] == 0) & (wave[None, :, None] == 0) & (wave[None, None, :] == 0)

    heat_filter = 1.0 + heat_time * laplace
    laplace_safe = jnp.where(anchor, 1.0, laplace)
    cas_x, cas_y = lax.optimization_barrier(
        (
            cas_columns(length, window_positions(length, count_x, 2)),
            cas_columns(length, window_positions(length, count_y, 4)),
        )
    )
    source = sources.astype(jnp.float32)
    spectrum = planes_forward(to_planes(source, cas), cas)
    padded = to_pencil_with_halo(spectrum / heat_filter * scale, cas, cas_x, cas_y)
    divergence = divergence_of_flow(padded[:, 2:-2], grad_floor)

    div_spectrum = planes_forward(to_planes(divergence, cas), cas)
    potential_spectrum = jnp.where(anchor, 0.0, -div_spectrum / laplace_safe) * scale
    potential = to_pencil(planes_inverse(potential_spectrum, cas), cas, count_x, count_y)
    signs = (2 * labels - 1).astype(jnp.float32)
    return signs * potential


def solution(mesh):
    return jax.shard_map(
        per_device,
        mesh=mesh,
        in_specs=(P("wide", "narrow", None), P("wide", "narrow", None)),
        out_specs=P("wide", "narrow", None),
        check_vma=False,
    )
```

profile of v0, /device:TPU:1, one launch (start us, length us, event | category | flops | bytes accessed | tf_op | source)
XLA Modules:
  0.0 115.3 jit_solution(10035405201585379833)
XLA Ops:
  0.0 2.5 %fusion.30 = f32[256,8,64]{0,2,1:T(8,128)S(1)} fusion(s32[8,64,256]{2,1,0:T(8,128)} %param.2), kind=kOutput, calls=%fused_computation.53 | convolution fusion | flops 202440704 | bytes 1048576 | tf_op jit(solution)/shard_map/xyz,zk->kxy/dot_general | solution.py:50
  2.5 0.4 copy.13
  2.9 1.0 reshape_reshape.18
  3.9 11.5 %all-to-all-start = ((f32[128,8,128]{2,1,0:T(8,128)}), f32[128,8,128]{2,1,0:T(8,128)S(1)}, u32[]{:S(2)}, u32[]{:S(2)}) async-start(f32[128,8,128]{2,1,0:T(8,128)} %reshape_reshape.18), calls=%async_computation | async-start | bytes 1048576 | tf_op jit(solution)/shard_map/all_to_all | solution.py:42
  15.4 1.6 %sine_add_fusion = f32[256,32,12]{0,1,2:T(8,128)S(1)} fusion(s32[32,12]{0,1:T(8,128)S(1)} %add_select_fusion.5), kind=kLoop, calls=%fused_computation.62 | loop fusion | flops 1474560 | bytes 394752 | tf_op jit(solution)/shard_map/add | solution.py:23
  17.1 0.1 add_select_fusion.6
  17.2 1.2 %sine_add_fusion.1 = f32[256,4,72]{0,2,1:T(8,128)S(1)} fusion(s32[4,72]{1,0:T(4,128)S(1)} %add_select_fusion.6), kind=kLoop, calls=%fused_computation.76 | loop fusion | flops 1105920 | bytes 296064 | tf_op jit(solution)/shard_map/add | solution.py:23
  18.5 0.1 broadcast_add_fusion
  18.6 10.3 %all-to-all-done = f32[128,8,128]{2,1,0:T(8,128)S(1)} async-done(((f32[128,8,128]{2,1,0:T(8,128)}), f32[128,8,128]{2,1,0:T(8,128)S(1)}, u32[]{:S(2)}, u32[]{:S(2)}) %all-to-all-start) | async-done | bytes 524320 | tf_op jit(solution)/shard_map/all_to_all | solution.py:42
  28.9 0.2 reshape_reshape.19
  29.2 1.9 %convolution_bitcast_fusion.5 = f32[2,32,8,256]{3,1,2,0:T(8,128)S(1)} fusion(f32[32,4,2,8,64]{4,3,2,1,0:T(8,128)S(1)} %reshape_reshape.19, s32[4,64]{1,0:T(4,128)S(1)} %multiply_add_fusion), kind=kOutput, calls=%fused_computation.8 | convolution fusion | flops 202309632 | bytes 1049600 | tf_op jit(solution)/shard_map/wqkxy,qyl->kwxl/dot_general | solution.py:53
  31.1 1.6 %fusion.3 = f32[2,256,256,1]{2,1,3,0:T(8,128)S(1)} fusion(f32[2,32,8,256]{3,1,2,0:T(8,128)S(1)} %convolution_bitcast_fusion.5, f32[2]{0:T(128)S(1)} %multiply_subtract_fusion.1, f32[256,256]{1,0:T(8,128)S(1)} %broadcast_add_fusion), kind=kOutput, calls=%fused_computation.11 | convolution fusion | flops 202964992 | bytes 1310728 | tf_op jit(solution)/shard_map/kxl,xm->kml/dot_general | solution.py:83
  32.7 0.5 convolution_bitcast_fusion.1
  33.2 0.8 convolution_bitcast_fusion
  34.0 0.9 copy.17
  35.0 2.2 %all_to_all.20 = f32[128,1,1728]{2,1,0:T(1,128)S(1)} reshape(f32[32,4,2,12,72]{4,3,2,1,0:T(8,128)S(1)} %copy.17) | data formatting | bytes 1769472 | tf_op jit(solution)/shard_map/all_to_all | solution.py:76
  37.2 22.0 %all_to_all.25 = f32[128,1,1728]{2,1,0:T(1,128)S(1)} all-to-all(f32[128,1,1728]{2,1,0:T(1,128)S(1)} %all_to_all.20), channel_id=1, replica_groups=mesh['wide'=32,'narrow'=4] {'wide','narrow'}, dimensions={0} | all-to-all | bytes 1769472 | tf_op jit(solution)/shard_map/all_to_all | solution.py:76
  59.2 2.2 %reduce = f32[128,1728]{1,0:T(8,128)S(1)} reduce(f32[128,1,1728]{2,1,0:T(1,128)S(1)} %all_to_all.25, f32[]{:T(128)} %constant.105), dimensions={1}, to_apply=%all_to_all.17.reduce_sub_computation | reduce | bytes 1769476 | tf_op jit(solution)/shard_map/all_to_all | solution.py:76
  61.4 0.2 reshape.279
  61.7 0.3 copy.19
  62.0 1.6 %fusion.59 = f32[12,72,256]{2,1,0:T(8,128)S(1)} fusion(f32[12,72,256]{2,1,0:T(8,128)S(1)} %bitcast.95), kind=kOutput, calls=%fused_computation.93 | convolution fusion | flops 340721664 | bytes 1769472 | tf_op jit(solution)/shard_map/kr,kz->rz/dot_general | solution.py:78
  63.5 0.3 fusion.119
  63.8 0.2 fusion.120
  64.0 0.8 negate_divide_fusion
  64.8 0.2 fusion.122
  65.0 0.1 fusion.121
  65.2 0.3 negate_divide_fusion.2
  65.5 1.7 %fusion.17 = f32[256,8,64]{0,2,1:T(8,128)S(1)} fusion(f32[10,66,256]{2,1,0:T(8,128)S(1)} %get-tuple-element.12, f32[10,66,256]{2,1,0:T(8,128)S(1)} %get-tuple-element.11, f32[8,64,1]{2,1,0:T(8,128)S(1)} %get-tuple-element.18, f32[8,64,255]{2,1,0:T(8,128)S(1)} %get-tuple-element.20, f32[8,64,255]{2,1,0:T(8,128)S(1)} %get-tuple-element.19, ...), kind=kOutput, calls=%fused_computation.39 | convolution fusion | flops 203358208 | bytes 4194304 | tf_op jit(solution)/shard_map/xyz,zk->kxy/dot_general | solution.py:50
  67.2 0.4 copy.20
  67.6 1.0 reshape_reshape.20
  68.6 4.7 %all-to-all-start.2 = ((f32[128,8,128]{2,1,0:T(8,128)}), f32[128,8,128]{2,1,0:T(8,128)S(1)}, u32[]{:S(2)}, u32[]{:S(2)}) async-start(f32[128,8,128]{2,1,0:T(8,128)} %reshape_reshape.20), calls=%async_computation.2 | async-start | bytes 1048576 | tf_op jit(solution)/shard_map/all_to_all | solution.py:42
  73.4 0.1 broadcast_and_fusion
  73.4 13.6 %all-to-all-done.2 = f32[128,8,128]{2,1,0:T(8,128)S(1)} async-done(((f32[128,8,128]{2,1,0:T(8,128)}), f32[128,8,128]{2,1,0:T(8,128)S(1)}, u32[]{:S(2)}, u32[]{:S(2)}) %all-to-all-start.2) | async-done | bytes 524320 | tf_op jit(solution)/shard_map/all_to_all | solution.py:42
  87.0 0.2 reshape_reshape.21
  87.2 1.9 %convolution_bitcast_fusion.3 = f32[2,32,8,256]{3,1,2,0:T(8,128)S(1)} fusion(f32[32,4,2,8,64]{4,3,2,1,0:T(8,128)S(1)} %reshape_reshape.21, s32[4,64]{1,0:T(4,128)S(1)} %multiply_add_fusion), kind=kOutput, calls=%fused_computation.6 | convolution fusion | flops 202309632 | bytes 1049600 | tf_op jit(solution)/shard_map/wqkxy,qyl->kwxl/dot_general | solution.py:53
  89.2 1.7 %fusion.6 = f32[2,256,256]{2,1,0:T(8,128)S(1)} fusion(f32[2,32,8,256]{3,1,2,0:T(8,128)S(1)} %convolution_bitcast_fusion.3, f32[2]{0:T(128)S(1)} %multiply_subtract_fusion.1, f32[256,256]{1,0:T(8,128)S(1)} %broadcast_add_fusion, pred[256]{0:T(512)(128)(4,1)S(1)} %iota_compare_fusion, pred[2,256]{1,0:T(4,128)(4,1)S(1)} %broadcast_and_fusion), kind=kOutput, calls=%fused_computation.14 | convolution fusion | flops 203227136 | bytes 1311496 | tf_op jit(solution)/shard_map/kxl,xm->kml/dot_general | solution.py:83
  90.9 1.5 %convolution_bitcast_fusion.2 = f32[2,256,256]{2,1,0:T(8,128)S(1)} fusion(f32[2,256,256]{2,1,0:T(8,128)S(1)} %fusion.6), kind=kOutput, calls=%fused_computation.3 | convolution fusion | flops 202309632 | bytes 1048576 | tf_op jit(solution)/shard_map/kml,mx->kxl/dot_general | solution.py:87
  92.4 1.4 %fusion.56 = f32[2,256,256]{2,1,0:T(8,128)S(1)} fusion(f32[2,256,256]{2,1,0:T(8,128)S(1)} %convolution_bitcast_fusion.2), kind=kOutput, calls=%fused_computation.90 | convolution fusion | flops 202309632 | bytes 1048576 | tf_op jit(solution)/shard_map/kxl,ly->kxy/dot_general | solution.py:88
  93.8 0.5 reshape.281
  94.3 0.1 copy.53
  94.3 0.2 reshape_reshape.22
  94.6 0.0 copy-start
  94.6 17.8 %all_to_all.26 = f32[128,8,128]{2,1,0:T(8,128)S(1)} all-to-all(f32[128,8,128]{2,1,0:T(8,128)S(1)} %reshape_reshape.22), channel_id=1, replica_groups=mesh['wide'=32,'narrow'=4] {'wide','narrow'}, dimensions={0} | all-to-all | bytes 1048576 | tf_op jit(solution)/shard_map/all_to_all | solution.py:42
  112.4 0.2 reshape_reshape.23
  112.6 0.0 copy-done
  112.6 2.7 %convolution_multiply_fusion = f32[8,64,256]{2,1,0:T(8,128)} fusion(f32[256,8,64]{2,1,0:T(8,128)S(1)} %reshape_reshape.23, s32[8,64,256]{2,1,0:T(8,128)S(1)} %copy-done), kind=kOutput, calls=%fused_computation.2 | convolution fusion | flops 202833920 | bytes 1572864 | tf_op jit(solution)/shard_map/kxy,kz->xyz/dot_general | solution.py:66
  (8 shorter events, 0.1 us)
Async XLA Ops:
  3.9 25.1 %all-to-all-start = ((f32[128,8,128]{2,1,0:T(8,128)}), f32[128,8,128]{2,1,0:T(8,128)S(1)}, u32[]{:S(2)}, u32[]{:S(2)}) async-start(f32[128,8,128]{2,1,0:T(8,128)} %reshape_reshape.18), calls=%async_computation | async-start | bytes 1048576 | tf_op jit(solution)/shard_map/all_to_all | solution.py:42
  68.6 18.4 %all-to-all-start.2 = ((f32[128,8,128]{2,1,0:T(8,128)}), f32[128,8,128]{2,1,0:T(8,128)S(1)}, u32[]{:S(2)}, u32[]{:S(2)}) async-start(f32[128,8,128]{2,1,0:T(8,128)} %reshape_reshape.20), calls=%async_computation.2 | async-start | bytes 1048576 | tf_op jit(solution)/shard_map/all_to_all | solution.py:42
  94.6 18.0 %copy-start = (s32[8,64,256]{2,1,0:T(8,128)S(1)}, s32[8,64,256]{2,1,0:T(8,128)}, u32[]{:S(2)}) copy-start(s32[8,64,256]{2,1,0:T(8,128)} %param.3) | copy-start | bytes 1572868
where the time goes:
time: 116 us; the launch traced here: 115 us
  blocking collectives  39.8 us (34%)
  waiting for transfers between devices  23.9 us (21%)
  matrix products  19.9 us (17%)
  starting transfers between devices  16.2 us (14%)
  local copies, waits for them, and re-layouts  8.69 us (7%)
  other arithmetic  6.59 us (6%)
    all_to_all x2, waiting for transfers between devices, exchange(): return lax.all_to_all(blocks, ALL, 0, 0).reshape(shape)  23.9 us
    all_to_all x1, blocking collectives, to_pencil_with_halo(): arrived = lax.all_to_all(send, ALL, 0, 0)  22 us
    all_to_all x1, blocking collectives, exchange(): return lax.all_to_all(blocks, ALL, 0, 0).reshape(shape)  17.8 us
    all_to_all x2, starting transfers between devices, exchange(): return lax.all_to_all(blocks, ALL, 0, 0).reshape(shape)  16.2 us
    dot_general x2, matrix products, to_planes(): along_z = jnp.einsum('xyz,zk->kxy', pencil, cas, precision=matmul_precision)  4.16 us
    dot_general x2, matrix products, to_planes(): jnp.einsum('wqkxy,qyl->kwxl', arrived, cas.reshape(narrow, count_y, lengt...  3.83 us
    dot_general x2, matrix products, planes_forward(): return jnp.einsum('kxl,xm->kml', along_y, cas, precision=matmul_precision)  3.36 us
    add x2, other arithmetic, cas_columns(): return jnp.cos(angles) + jnp.sin(angles)  2.87 us
  transfers between devices with their start and end apart: 2, of which 2 were waited for; matrix products, arithmetic and copies ran while one was open for 3% of the time, Pallas kernels for 0%

commit v1 on v0

--- a/solution.py
+++ b/solution.py
@@ -37,9 +37,12 @@
 def exchange(blocks):
     shape = blocks.shape
     size = math.prod(shape[1:])
-    if size % 1024 == 0:
-        blocks = blocks.reshape(shape[0], size // 128, 128)
-    return lax.all_to_all(blocks, ALL, 0, 0).reshape(shape)
+    tiles = -(-size // 1024)
+    flat = blocks.reshape(shape[0], size)
+    if tiles * 1024 != size:
+        flat = jnp.pad(flat, ((0, 0), (0, tiles * 1024 - size)))
+    arrived = lax.all_to_all(flat.reshape(shape[0], tiles * 8, 128), ALL, 0, 0)
+    return arrived.reshape(shape[0], tiles * 1024)[:, :size].reshape(shape)
 
 
 def to_planes(pencil, cas):
@@ -72,8 +75,7 @@
     _, narrow, padded_y = cas_y.shape
     along_x = jnp.einsum("kml,mwi->kwil", spectrum, cas_x, precision=matmul_precision)
     windows = jnp.einsum("kwil,lqj->wqkij", along_x, cas_y, precision=matmul_precision)
-    send = windows.reshape(wide * narrow, span * padded_x * padded_y)
-    arrived = lax.all_to_all(send, ALL, 0, 0)
+    arrived = exchange(windows.reshape(wide * narrow, span * padded_x * padded_y))
     spectrum_z = arrived.reshape(wide * narrow * span, padded_x * padded_y)
     values = jnp.einsum("kr,kz->rz", spectrum_z, cas, precision=matmul_precision)
     return values.reshape(padded_x, padded_y, length)

time: 116 us -> 114 us (0.983)
  other arithmetic: 6.59 us -> 4.41 us
  blocking collectives: 39.8 us -> 41 us
    all_to_all x1 -> x0, local copies, waits for them, and re-layouts: 2.25 us -> none  [to_pencil_with_halo(): arrived = lax.all_to_all(send, ALL, 0, 0)]
    all_to_all x1 -> x0, other arithmetic: 2.18 us -> none  [to_pencil_with_halo(): arrived = lax.all_to_all(send, ALL, 0, 0)]
    all_to_all x2, blocking collectives: 39.8 us -> 41 us  [exchange(): arrived = lax.all_to_all(flat.reshape(shape[0], tiles * 8, 128), ALL, 0, 0)]
where the time goes in v1:
time: 114 us
  blocking collectives  41 us (36%)
  waiting for transfers between devices  23.9 us (21%)
  matrix products  19.9 us (17%)
  starting transfers between devices  16.2 us (14%)
  local copies, waits for them, and re-layouts  8.22 us (7%)
  other arithmetic  4.41 us (4%)
    all_to_all x2, blocking collectives, exchange(): arrived = lax.all_to_all(flat.reshape(shape[0], tiles * 8, 128), ALL, 0, 0)  41 us
    all_to_all x2, waiting for transfers between devices, exchange(): arrived = lax.all_to_all(flat.reshape(shape[0], tiles * 8, 128), ALL, 0, 0)  23.9 us
    all_to_all x2, starting transfers between devices, exchange(): arrived = lax.all_to_all(flat.reshape(shape[0], tiles * 8, 128), ALL, 0, 0)  16.2 us
    dot_general x2, matrix products, to_planes(): along_z = jnp.einsum('xyz,zk->kxy', pencil, cas, precision=matmul_precision)  4.16 us
    dot_general x2, matrix products, to_planes(): jnp.einsum('wqkxy,qyl->kwxl', arrived, cas.reshape(narrow, count_y, lengt...  3.83 us
    dot_general x2, matrix products, planes_forward(): return jnp.einsum('kxl,xm->kml', along_y, cas, precision=matmul_precision)  3.36 us
    add x2, other arithmetic, cas_columns(): return jnp.cos(angles) + jnp.sin(angles)  2.87 us
    dot_general x1, matrix products, to_pencil(): return jnp.einsum('kxy,kz->xyz', spectrum, cas, precision=matmul_precision)  2.74 us
  transfers between devices with their start and end apart: 2, of which 2 were waited for; matrix products, arithmetic and copies ran while one was open for 3% of the time, Pallas kernels for 0%

profile of v1, /device:TPU:1, one launch (start us, length us, event | category | flops | bytes accessed | tf_op | source)
XLA Modules:
  0.0 113.9 jit_solution(14563454799195562177)
XLA Ops:
  0.0 2.5 %fusion.30 = f32[256,8,64]{0,2,1:T(8,128)S(1)} fusion(s32[8,64,256]{2,1,0:T(8,128)} %param.2), kind=kOutput, calls=%fused_computation.55 | convolution fusion | flops 202440704 | bytes 1048576 | tf_op jit(solution)/shard_map/xyz,zk->kxy/dot_general | solution.py:53
  2.5 0.4 copy.13
  2.9 1.0 reshape_reshape_reshape.18
  3.9 11.5 %all-to-all-start = ((f32[128,8,128]{2,1,0:T(8,128)}), f32[128,8,128]{2,1,0:T(8,128)S(1)}, u32[]{:S(2)}, u32[]{:S(2)}) async-start(f32[128,8,128]{2,1,0:T(8,128)} %reshape_reshape_reshape.18), calls=%async_computation | async-start | bytes 1048576 | tf_op jit(solution)/shard_map/all_to_all | solution.py:44
  15.4 1.6 %sine_add_fusion = f32[256,32,12]{0,1,2:T(8,128)S(1)} fusion(s32[32,12]{0,1:T(8,128)S(1)} %add_select_fusion.5), kind=kLoop, calls=%fused_computation.64 | loop fusion | flops 1474560 | bytes 394752 | tf_op jit(solution)/shard_map/add | solution.py:23
  17.1 0.1 add_select_fusion.6
  17.2 1.2 %sine_add_fusion.1 = f32[256,4,72]{0,2,1:T(8,128)S(1)} fusion(s32[4,72]{1,0:T(4,128)S(1)} %add_select_fusion.6), kind=kLoop, calls=%fused_computation.78 | loop fusion | flops 1105920 | bytes 296064 | tf_op jit(solution)/shard_map/add | solution.py:23
  18.5 0.1 broadcast_add_fusion
  18.6 10.3 %all-to-all-done = f32[128,8,128]{2,1,0:T(8,128)S(1)} async-done(((f32[128,8,128]{2,1,0:T(8,128)}), f32[128,8,128]{2,1,0:T(8,128)S(1)}, u32[]{:S(2)}, u32[]{:S(2)}) %all-to-all-start) | async-done | bytes 524320 | tf_op jit(solution)/shard_map/all_to_all | solution.py:44
  28.9 0.2 reshape_reshape_reshape.19
  29.2 1.9 %convolution_bitcast_fusion.5 = f32[2,32,8,256]{3,1,2,0:T(8,128)S(1)} fusion(f32[32,4,2,8,64]{4,3,2,1,0:T(8,128)S(1)} %reshape_reshape_reshape.19, s32[4,64]{1,0:T(4,128)S(1)} %multiply_add_fusion), kind=kOutput, calls=%fused_computation.8 | convolution fusion | flops 202309632 | bytes 1049600 | tf_op jit(solution)/shard_map/wqkxy,qyl->kwxl/dot_general | solution.py:56
  31.1 1.6 %fusion.3 = f32[2,256,256,1]{2,1,3,0:T(8,128)S(1)} fusion(f32[2,32,8,256]{3,1,2,0:T(8,128)S(1)} %convolution_bitcast_fusion.5, f32[2]{0:T(128)S(1)} %multiply_subtract_fusion.1, f32[256,256]{1,0:T(8,128)S(1)} %broadcast_add_fusion), kind=kOutput, calls=%fused_computation.11 | convolution fusion | flops 202964992 | bytes 1310728 | tf_op jit(solution)/shard_map/kxl,xm->kml/dot_general | solution.py:85
  32.7 0.5 convolution_bitcast_fusion.1
  33.2 0.8 convolution_bitcast_fusion
  34.0 0.9 copy.17
  35.0 1.1 reshape.283
  36.1 0.1 pad_bitcast_fusion
  36.2 0.2 copy.37
  36.4 23.1 %all_to_all.20 = f32[128,16,128]{2,1,0:T(8,128)S(1)} all-to-all(f32[128,16,128]{2,1,0:T(8,128)S(1)} %bitcast.100), channel_id=1, replica_groups=mesh['wide'=32,'narrow'=4] {'wide','narrow'}, dimensions={0} | all-to-all | bytes 2097152 | tf_op jit(solution)/shard_map/all_to_all | solution.py:44
  59.5 0.3 copy.55
  59.9 0.1 slice.92
  59.9 0.2 reshape.286
  60.2 0.3 copy.18
  60.5 1.6 %fusion.59 = f32[12,72,256]{2,1,0:T(8,128)S(1)} fusion(f32[12,72,256]{2,1,0:T(8,128)S(1)} %bitcast.105), kind=kOutput, calls=%fused_computation.95 | convolution fusion | flops 340721664 | bytes 1769472 | tf_op jit(solution)/shard_map/kr,kz->rz/dot_general | solution.py:80
  62.1 0.3 fusion.119
  62.3 0.2 fusion.120
  62.5 0.8 negate_divide_fusion
  63.3 0.2 fusion.122
  63.6 0.1 fusion.121
  63.7 0.3 negate_divide_fusion.2
  64.0 1.7 %fusion.17 = f32[256,8,64]{0,2,1:T(8,128)S(1)} fusion(f32[10,66,256]{2,1,0:T(8,128)S(1)} %get-tuple-element.12, f32[10,66,256]{2,1,0:T(8,128)S(1)} %get-tuple-element.11, f32[8,64,1]{2,1,0:T(8,128)S(1)} %get-tuple-element.18, f32[8,64,255]{2,1,0:T(8,128)S(1)} %get-tuple-element.20, f32[8,64,255]{2,1,0:T(8,128)S(1)} %get-tuple-element.19, ...), kind=kOutput, calls=%fused_computation.41 | convolution fusion | flops 203358208 | bytes 4194304 | tf_op jit(solution)/shard_map/xyz,zk->kxy/dot_general | solution.py:53
  65.7 0.4 copy.19
  66.2 1.0 reshape_reshape_reshape.20
  67.1 4.7 %all-to-all-start.2 = ((f32[128,8,128]{2,1,0:T(8,128)}), f32[128,8,128]{2,1,0:T(8,128)S(1)}, u32[]{:S(2)}, u32[]{:S(2)}) async-start(f32[128,8,128]{2,1,0:T(8,128)} %reshape_reshape_reshape.20), calls=%async_computation.2 | async-start | bytes 1048576 | tf_op jit(solution)/shard_map/all_to_all | solution.py:44
  71.9 0.1 broadcast_and_fusion
  72.0 13.6 %all-to-all-done.2 = f32[128,8,128]{2,1,0:T(8,128)S(1)} async-done(((f32[128,8,128]{2,1,0:T(8,128)}), f32[128,8,128]{2,1,0:T(8,128)S(1)}, u32[]{:S(2)}, u32[]{:S(2)}) %all-to-all-start.2) | async-done | bytes 524320 | tf_op jit(solution)/shard_map/all_to_all | solution.py:44
  85.6 0.2 reshape_reshape_reshape.21
  85.8 1.9 %convolution_bitcast_fusion.3 = f32[2,32,8,256]{3,1,2,0:T(8,128)S(1)} fusion(f32[32,4,2,8,64]{4,3,2,1,0:T(8,128)S(1)} %reshape_reshape_reshape.21, s32[4,64]{1,0:T(4,128)S(1)} %multiply_add_fusion), kind=kOutput, calls=%fused_computation.6 | convolution fusion | flops 202309632 | bytes 1049600 | tf_op jit(solution)/shard_map/wqkxy,qyl->kwxl/dot_general | solution.py:56
  87.7 1.7 %fusion.6 = f32[2,256,256]{2,1,0:T(8,128)S(1)} fusion(f32[2,32,8,256]{3,1,2,0:T(8,128)S(1)} %convolution_bitcast_fusion.3, f32[2]{0:T(128)S(1)} %multiply_subtract_fusion.1, f32[256,256]{1,0:T(8,128)S(1)} %broadcast_add_fusion, pred[256]{0:T(512)(128)(4,1)S(1)} %iota_compare_fusion, pred[2,256]{1,0:T(4,128)(4,1)S(1)} %broadcast_and_fusion), kind=kOutput, calls=%fused_computation.14 | convolution fusion | flops 203227136 | bytes 1311496 | tf_op jit(solution)/shard_map/kxl,xm->kml/dot_general | solution.py:85
  89.4 1.5 %convolution_bitcast_fusion.2 = f32[2,256,256]{2,1,0:T(8,128)S(1)} fusion(f32[2,256,256]{2,1,0:T(8,128)S(1)} %fusion.6), kind=kOutput, calls=%fused_computation.3 | convolution fusion | flops 202309632 | bytes 1048576 | tf_op jit(solution)/shard_map/kml,mx->kxl/dot_general | solution.py:89
  90.9 1.4 %fusion.56 = f32[2,256,256]{2,1,0:T(8,128)S(1)} fusion(f32[2,256,256]{2,1,0:T(8,128)S(1)} %convolution_bitcast_fusion.2), kind=kOutput, calls=%fused_computation.92 | convolution fusion | flops 202309632 | bytes 1048576 | tf_op jit(solution)/shard_map/kxl,ly->kxy/dot_general | solution.py:90
  92.3 0.5 reshape.288
  92.8 0.1 copy.56
  92.9 0.2 reshape_reshape_reshape.22
  93.1 0.0 copy-start
  93.1 17.8 %all_to_all.21 = f32[128,8,128]{2,1,0:T(8,128)S(1)} all-to-all(f32[128,8,128]{2,1,0:T(8,128)S(1)} %reshape_reshape_reshape.22), channel_id=1, replica_groups=mesh['wide'=32,'narrow'=4] {'wide','narrow'}, dimensions={0} | all-to-all | bytes 1048576 | tf_op jit(solution)/shard_map/all_to_all | solution.py:44
  110.9 0.2 reshape_reshape_reshape.23
  111.1 2.7 %convolution_multiply_fusion = f32[8,64,256]{2,1,0:T(8,128)} fusion(f32[256,8,64]{2,1,0:T(8,128)S(1)} %reshape_reshape_reshape.23, s32[8,64,256]{2,1,0:T(8,128)S(1)} %copy-done), kind=kOutput, calls=%fused_computation.2 | convolution fusion | flops 202833920 | bytes 1572864 | tf_op jit(solution)/shard_map/kxy,kz->xyz/dot_general | solution.py:69
  (9 shorter events, 0.1 us)
Async XLA Ops:
  3.9 25.1 %all-to-all-start = ((f32[128,8,128]{2,1,0:T(8,128)}), f32[128,8,128]{2,1,0:T(8,128)S(1)}, u32[]{:S(2)}, u32[]{:S(2)}) async-start(f32[128,8,128]{2,1,0:T(8,128)} %reshape_reshape_reshape.18), calls=%async_computation | async-start | bytes 1048576 | tf_op jit(solution)/shard_map/all_to_all | solution.py:44
  67.1 18.4 %all-to-all-start.2 = ((f32[128,8,128]{2,1,0:T(8,128)}), f32[128,8,128]{2,1,0:T(8,128)S(1)}, u32[]{:S(2)}, u32[]{:S(2)}) async-start(f32[128,8,128]{2,1,0:T(8,128)} %reshape_reshape_reshape.20), calls=%async_computation.2 | async-start | bytes 1048576 | tf_op jit(solution)/shard_map/all_to_all | solution.py:44
  93.1 18.0 %copy-start = (s32[8,64,256]{2,1,0:T(8,128)S(1)}, s32[8,64,256]{2,1,0:T(8,128)}, u32[]{:S(2)}) copy-start(s32[8,64,256]{2,1,0:T(8,128)} %param.3) | copy-start | bytes 1572868

commit v2 on v1

--- a/solution.py
+++ b/solution.py
@@ -126,8 +126,9 @@
 
     heat_filter = 1.0 + heat_time * laplace
     laplace_safe = jnp.where(anchor, 1.0, laplace)
-    cas_x, cas_y = lax.optimization_barrier(
+    cas, cas_x, cas_y = lax.optimization_barrier(
         (
+            cas,
             cas_columns(length, window_positions(length, count_x, 2)),
             cas_columns(length, window_positions(length, count_y, 4)),
         )

time: 114 us -> 109 us (0.956)
  matrix products: 19.9 us -> 10.1 us
  waiting for transfers between devices: 23.9 us -> 26.9 us
    all_to_all x2, waiting for transfers between devices: 23.9 us -> 26.9 us  [exchange(): arrived = lax.all_to_all(flat.reshape(shape[0], tiles * 8, 128), ALL, 0, 0)]
    dot_general x2, matrix products: 4.16 us -> 2.08 us  [to_planes(): along_z = jnp.einsum('xyz,zk->kxy', pencil, cas, precision=matmul_precision)]
    dot_general x2, matrix products: 3.36 us -> 1.54 us  [planes_forward(): return jnp.einsum('kxl,xm->kml', along_y, cas, precision=matmul_precision)]
    dot_general x2, matrix products: 3.83 us -> 2.12 us  [to_planes(): jnp.einsum('wqkxy,qyl->kwxl', arrived, cas.reshape(narrow, count_y, lengt...]
  transfers between devices with their start and end apart: 2 -> 2, of which waited for: 2 -> 2; matrix products, arithmetic and copies ran while one was open for 3% -> 0% of each run, Pallas kernels for 0% -> 0%
where the time goes in v2:
time: 109 us; the launch traced here: 108 us
  blocking collectives  41.1 us (38%)
  waiting for transfers between devices  26.9 us (25%)
  starting transfers between devices  16.2 us (15%)
  matrix products  10.1 us (9%)
  local copies, waits for them, and re-layouts  8.22 us (8%)
  other arithmetic  5.45 us (5%)
    all_to_all x2, blocking collectives, exchange(): arrived = lax.all_to_all(flat.reshape(shape[0], tiles * 8, 128), ALL, 0, 0)  41.1 us
    all_to_all x2, waiting for transfers between devices, exchange(): arrived = lax.all_to_all(flat.reshape(shape[0], tiles * 8, 128), ALL, 0, 0)  26.9 us
    all_to_all x2, starting transfers between devices, exchange(): arrived = lax.all_to_all(flat.reshape(shape[0], tiles * 8, 128), ALL, 0, 0)  16.2 us
    add x2, other arithmetic, cas_columns(): return jnp.cos(angles) + jnp.sin(angles)  2.87 us
    another operation x3, local copies, waits for them, and re-layouts, exchange(): arrived = lax.all_to_all(flat.reshape(shape[0], tiles * 8, 128), ALL, 0, 0)  2.2 us
  transfers between devices with their start and end apart: 2, of which 2 were waited for; matrix products, arithmetic and copies ran while one was open for 0% of the time, Pallas kernels for 0%

profile of v2, /device:TPU:1, one launch (start us, length us, event | category | flops | bytes accessed | tf_op | source)
XLA Modules:
  0.0 108.4 jit_solution(3578578295787343825)
XLA Ops:
  0.0 1.0 sine_add_fusion.2
  1.1 1.6 %sine_add_fusion = f32[256,32,12]{0,1,2:T(8,128)S(1)} fusion(s32[32,12]{0,1:T(8,128)S(1)} %add_select_fusion.4), kind=kLoop, calls=%fused_computation.64 | loop fusion | flops 1474560 | bytes 394752 | tf_op jit(solution)/shard_map/add | solution.py:23
  2.7 0.1 add_select_fusion.5
  2.8 1.2 %sine_add_fusion.1 = f32[256,4,72]{0,2,1:T(8,128)S(1)} fusion(s32[4,72]{1,0:T(4,128)S(1)} %add_select_fusion.5), kind=kLoop, calls=%fused_computation.75 | loop fusion | flops 1105920 | bytes 296064 | tf_op jit(solution)/shard_map/add | solution.py:23
  4.0 1.4 %fusion.30 = f32[256,8,64]{0,2,1:T(8,128)S(1)} fusion(s32[8,64,256]{2,1,0:T(8,128)} %param.2, f32[256,256]{1,0:T(8,128)S(1)} %sine_add_fusion.2), kind=kOutput, calls=%fused_computation.55 | convolution fusion | flops 201457664 | bytes 1310720 | tf_op jit(solution)/shard_map/xyz,zk->kxy/dot_general | solution.py:53
  5.5 0.4 copy.13
  5.9 1.0 reshape_reshape_reshape.18
  6.9 11.5 %all-to-all-start = ((f32[128,8,128]{2,1,0:T(8,128)}), f32[128,8,128]{2,1,0:T(8,128)S(1)}, u32[]{:S(2)}, u32[]{:S(2)}) async-start(f32[128,8,128]{2,1,0:T(8,128)} %reshape_reshape_reshape.18), calls=%async_computation | async-start | bytes 1048576 | tf_op jit(solution)/shard_map/all_to_all | solution.py:44
  18.5 0.1 broadcast_add_fusion
  18.6 13.3 %all-to-all-done = f32[128,8,128]{2,1,0:T(8,128)S(1)} async-done(((f32[128,8,128]{2,1,0:T(8,128)}), f32[128,8,128]{2,1,0:T(8,128)S(1)}, u32[]{:S(2)}, u32[]{:S(2)}) %all-to-all-start) | async-done | bytes 524320 | tf_op jit(solution)/shard_map/all_to_all | solution.py:44
  31.9 0.2 reshape_reshape_reshape.19
  32.2 1.1 convolution_bitcast_fusion.5
  33.2 0.7 fusion.3
  33.9 0.5 convolution_bitcast_fusion.1
  34.4 0.8 convolution_bitcast_fusion
  35.3 0.9 copy.17
  36.2 1.1 reshape.208
  37.3 0.1 pad_bitcast_fusion
  37.4 0.2 copy.37
  37.6 23.3 %all_to_all.20 = f32[128,16,128]{2,1,0:T(8,128)S(1)} all-to-all(f32[128,16,128]{2,1,0:T(8,128)S(1)} %bitcast.100), channel_id=1, replica_groups=mesh['wide'=32,'narrow'=4] {'wide','narrow'}, dimensions={0} | all-to-all | bytes 2097152 | tf_op jit(solution)/shard_map/all_to_all | solution.py:44
  60.9 0.3 copy.55
  61.3 0.1 slice.92
  61.3 0.2 reshape.211
  61.6 0.3 copy.18
  61.9 0.5 fusion.54
  62.4 0.3 fusion.71
  62.7 0.2 fusion.72
  62.9 0.8 negate_divide_fusion
  63.7 0.2 fusion.74
  63.9 0.1 fusion.73
  64.0 0.3 negate_divide_fusion.2
  64.4 0.6 fusion.17
  65.0 0.4 copy.19
  65.5 1.0 reshape_reshape_reshape.20
  66.5 4.7 %all-to-all-start.2 = ((f32[128,8,128]{2,1,0:T(8,128)}), f32[128,8,128]{2,1,0:T(8,128)S(1)}, u32[]{:S(2)}, u32[]{:S(2)}) async-start(f32[128,8,128]{2,1,0:T(8,128)} %reshape_reshape_reshape.20), calls=%async_computation.2 | async-start | bytes 1048576 | tf_op jit(solution)/shard_map/all_to_all | solution.py:44
  71.2 0.1 broadcast_and_fusion
  71.3 13.6 %all-to-all-done.2 = f32[128,8,128]{2,1,0:T(8,128)S(1)} async-done(((f32[128,8,128]{2,1,0:T(8,128)}), f32[128,8,128]{2,1,0:T(8,128)S(1)}, u32[]{:S(2)}, u32[]{:S(2)}) %all-to-all-start.2) | async-done | bytes 524320 | tf_op jit(solution)/shard_map/all_to_all | solution.py:44
  84.9 0.2 reshape_reshape_reshape.21
  85.1 1.1 convolution_bitcast_fusion.3
  86.2 0.8 fusion.6
  87.0 0.4 convolution_bitcast_fusion.2
  87.4 0.4 fusion.51
  87.8 0.5 reshape.213
  88.3 0.1 copy.56
  88.3 0.2 reshape_reshape_reshape.22
  88.6 17.8 %all_to_all.21 = f32[128,8,128]{2,1,0:T(8,128)S(1)} all-to-all(f32[128,8,128]{2,1,0:T(8,128)S(1)} %reshape_reshape_reshape.22), channel_id=1, replica_groups=mesh['wide'=32,'narrow'=4] {'wide','narrow'}, dimensions={0} | all-to-all | bytes 1048576 | tf_op jit(solution)/shard_map/all_to_all | solution.py:44
  106.4 0.2 reshape_reshape_reshape.23
  106.6 1.8 %convolution_multiply_fusion = f32[8,64,256]{2,1,0:T(8,128)} fusion(f32[256,8,64]{2,1,0:T(8,128)S(1)} %reshape_reshape_reshape.23, s32[8,64,256]{2,1,0:T(8,128)S(1)} %copy-done, f32[256,256]{1,0:T(8,128)S(1)} %sine_add_fusion.2), kind=kOutput, calls=%fused_computation.2 | convolution fusion | flops 201850880 | bytes 1835008 | tf_op jit(solution)/shard_map/kxy,kz->xyz/dot_general | solution.py:69
  (9 shorter events, 0.1 us)
Async XLA Ops:
  6.9 25.1 %all-to-all-start = ((f32[128,8,128]{2,1,0:T(8,128)}), f32[128,8,128]{2,1,0:T(8,128)S(1)}, u32[]{:S(2)}, u32[]{:S(2)}) async-start(f32[128,8,128]{2,1,0:T(8,128)} %reshape_reshape_reshape.18), calls=%async_computation | async-start | bytes 1048576 | tf_op jit(solution)/shard_map/all_to_all | solution.py:44
  66.5 18.4 %all-to-all-start.2 = ((f32[128,8,128]{2,1,0:T(8,128)}), f32[128,8,128]{2,1,0:T(8,128)S(1)}, u32[]{:S(2)}, u32[]{:S(2)}) async-start(f32[128,8,128]{2,1,0:T(8,128)} %reshape_reshape_reshape.20), calls=%async_computation.2 | async-start | bytes 1048576 | tf_op jit(solution)/shard_map/all_to_all | solution.py:44
  88.6 18.0 %copy-start = (s32[8,64,256]{2,1,0:T(8,128)S(1)}, s32[8,64,256]{2,1,0:T(8,128)}, u32[]{:S(2)}) copy-start(s32[8,64,256]{2,1,0:T(8,128)} %param.3) | copy-start | bytes 1572868

commit v3 on v1

--- a/solution.py
+++ b/solution.py
@@ -126,6 +126,7 @@
 
     heat_filter = 1.0 + heat_time * laplace
     laplace_safe = jnp.where(anchor, 1.0, laplace)
+    cas = lax.optimization_barrier(cas)
     cas_x, cas_y = lax.optimization_barrier(
         (
             cas_columns(length, window_positions(length, count_x, 2)),

time: 114 us -> 106 us (0.930)
  matrix products: 19.9 us -> 10.2 us
    dot_general x2, matrix products: 4.16 us -> 2.08 us  [to_planes(): along_z = jnp.einsum('xyz,zk->kxy', pencil, cas, precision=matmul_precision)]
    dot_general x2, matrix products: 3.36 us -> 1.55 us  [planes_forward(): return jnp.einsum('kxl,xm->kml', along_y, cas, precision=matmul_precision)]
    dot_general x2, matrix products: 3.83 us -> 2.12 us  [to_planes(): jnp.einsum('wqkxy,qyl->kwxl', arrived, cas.reshape(narrow, count_y, lengt...]
where the time goes in v3:
time: 106 us; the launch traced here: 105 us
  blocking collectives  41.1 us (39%)
  waiting for transfers between devices  23.9 us (23%)
  starting transfers between devices  16.2 us (15%)
  matrix products  10.2 us (10%)
  local copies, waits for them, and re-layouts  8.22 us (8%)
  other arithmetic  5.45 us (5%)
    all_to_all x2, blocking collectives, exchange(): arrived = lax.all_to_all(flat.reshape(shape[0], tiles * 8, 128), ALL, 0, 0)  41.1 us
    all_to_all x2, waiting for transfers between devices, exchange(): arrived = lax.all_to_all(flat.reshape(shape[0], tiles * 8, 128), ALL, 0, 0)  23.9 us
    all_to_all x2, starting transfers between devices, exchange(): arrived = lax.all_to_all(flat.reshape(shape[0], tiles * 8, 128), ALL, 0, 0)  16.2 us
    add x2, other arithmetic, cas_columns(): return jnp.cos(angles) + jnp.sin(angles)  2.87 us
    another operation x3, local copies, waits for them, and re-layouts, exchange(): arrived = lax.all_to_all(flat.reshape(shape[0], tiles * 8, 128), ALL, 0, 0)  2.2 us
    dot_general x2, matrix products, to_planes(): jnp.einsum('wqkxy,qyl->kwxl', arrived, cas.reshape(narrow, count_y, lengt...  2.12 us
  transfers between devices with their start and end apart: 2, of which 2 were waited for; matrix products, arithmetic and copies ran while one was open for 3% of the time, Pallas kernels for 0%

profile of v3, /device:TPU:1, one launch (start us, length us, event | category | flops | bytes accessed | tf_op | source)
XLA Modules:
  0.0 105.4 jit_solution(17883681930188545921)
XLA Ops:
  0.0 1.0 sine_add_fusion.2
  1.0 1.4 %fusion.30 = f32[256,8,64]{0,2,1:T(8,128)S(1)} fusion(s32[8,64,256]{2,1,0:T(8,128)} %param.2, f32[256,256]{1,0:T(8,128)S(1)} %sine_add_fusion.2), kind=kOutput, calls=%fused_computation.55 | convolution fusion | flops 201457664 | bytes 1310720 | tf_op jit(solution)/shard_map/xyz,zk->kxy/dot_general | solution.py:53
  2.5 0.4 copy.13
  2.9 1.0 reshape_reshape_reshape.18
  3.9 11.5 %all-to-all-start = ((f32[128,8,128]{2,1,0:T(8,128)}), f32[128,8,128]{2,1,0:T(8,128)S(1)}, u32[]{:S(2)}, u32[]{:S(2)}) async-start(f32[128,8,128]{2,1,0:T(8,128)} %reshape_reshape_reshape.18), calls=%async_computation | async-start | bytes 1048576 | tf_op jit(solution)/shard_map/all_to_all | solution.py:44
  15.4 1.6 %sine_add_fusion = f32[256,32,12]{0,1,2:T(8,128)S(1)} fusion(s32[32,12]{0,1:T(8,128)S(1)} %add_select_fusion.4), kind=kLoop, calls=%fused_computation.64 | loop fusion | flops 1474560 | bytes 394752 | tf_op jit(solution)/shard_map/add | solution.py:23
  17.1 0.1 add_select_fusion.5
  17.1 1.2 %sine_add_fusion.1 = f32[256,4,72]{0,2,1:T(8,128)S(1)} fusion(s32[4,72]{1,0:T(4,128)S(1)} %add_select_fusion.5), kind=kLoop, calls=%fused_computation.75 | loop fusion | flops 1105920 | bytes 296064 | tf_op jit(solution)/shard_map/add | solution.py:23
  18.5 0.1 broadcast_add_fusion
  18.6 10.3 %all-to-all-done = f32[128,8,128]{2,1,0:T(8,128)S(1)} async-done(((f32[128,8,128]{2,1,0:T(8,128)}), f32[128,8,128]{2,1,0:T(8,128)S(1)}, u32[]{:S(2)}, u32[]{:S(2)}) %all-to-all-start) | async-done | bytes 524320 | tf_op jit(solution)/shard_map/all_to_all | solution.py:44
  29.0 0.2 reshape_reshape_reshape.19
  29.2 1.1 %convolution_bitcast_fusion.5 = f32[2,32,8,256]{3,1,2,0:T(8,128)S(1)} fusion(f32[4,64,256,1,1]{2,1,0,4,3:T(8,128)S(1)} %bitcast.98, f32[32,4,2,8,64]{4,3,2,1,0:T(8,128)S(1)} %reshape_reshape_reshape.19), kind=kOutput, calls=%fused_computation.8 | convolution fusion | flops 201326592 | bytes 1310720 | tf_op jit(solution)/shard_map/wqkxy,qyl->kwxl/dot_general | solution.py:56
  30.2 0.7 fusion.3
  30.9 0.5 convolution_bitcast_fusion.1
  31.4 0.8 convolution_bitcast_fusion
  32.3 0.9 copy.17
  33.2 1.1 %reshape.208 = f32[128,1728]{1,0:T(8,128)S(1)} reshape(f32[32,4,2,12,72]{4,3,2,1,0:T(8,128)S(1)} %copy.17) | data formatting | bytes 1769472 | tf_op jit(solution)/shard_map/reshape | solution.py:78
  34.3 0.1 pad_bitcast_fusion
  34.4 0.2 copy.37
  34.6 23.3 %all_to_all.20 = f32[128,16,128]{2,1,0:T(8,128)S(1)} all-to-all(f32[128,16,128]{2,1,0:T(8,128)S(1)} %bitcast.100), channel_id=1, replica_groups=mesh['wide'=32,'narrow'=4] {'wide','narrow'}, dimensions={0} | all-to-all | bytes 2097152 | tf_op jit(solution)/shard_map/all_to_all | solution.py:44
  57.9 0.3 copy.55
  58.3 0.1 slice.92
  58.3 0.2 reshape.211
  58.6 0.3 copy.18
  58.9 0.5 fusion.54
  59.4 0.3 fusion.71
  59.7 0.2 fusion.72
  59.9 0.8 negate_divide_fusion
  60.7 0.2 fusion.74
  60.9 0.1 fusion.73
  61.1 0.3 negate_divide_fusion.2
  61.4 0.6 fusion.17
  62.0 0.4 copy.19
  62.5 1.0 reshape_reshape_reshape.20
  63.5 4.7 %all-to-all-start.2 = ((f32[128,8,128]{2,1,0:T(8,128)}), f32[128,8,128]{2,1,0:T(8,128)S(1)}, u32[]{:S(2)}, u32[]{:S(2)}) async-start(f32[128,8,128]{2,1,0:T(8,128)} %reshape_reshape_reshape.20), calls=%async_computation.2 | async-start | bytes 1048576 | tf_op jit(solution)/shard_map/all_to_all | solution.py:44
  68.2 0.1 broadcast_and_fusion
  68.3 13.6 %all-to-all-done.2 = f32[128,8,128]{2,1,0:T(8,128)S(1)} async-done(((f32[128,8,128]{2,1,0:T(8,128)}), f32[128,8,128]{2,1,0:T(8,128)S(1)}, u32[]{:S(2)}, u32[]{:S(2)}) %all-to-all-start.2) | async-done | bytes 524320 | tf_op jit(solution)/shard_map/all_to_all | solution.py:44
  81.9 0.2 reshape_reshape_reshape.21
  82.1 1.1 %convolution_bitcast_fusion.3 = f32[2,32,8,256]{3,1,2,0:T(8,128)S(1)} fusion(f32[4,64,256,1,1]{2,1,0,4,3:T(8,128)S(1)} %bitcast.99, f32[32,4,2,8,64]{4,3,2,1,0:T(8,128)S(1)} %reshape_reshape_reshape.21), kind=kOutput, calls=%fused_computation.6 | convolution fusion | flops 201326592 | bytes 1310720 | tf_op jit(solution)/shard_map/wqkxy,qyl->kwxl/dot_general | solution.py:56
  83.2 0.8 fusion.6
  84.0 0.4 convolution_bitcast_fusion.2
  84.5 0.4 fusion.51
  84.8 0.5 reshape.213
  85.3 0.1 copy.56
  85.4 0.2 reshape_reshape_reshape.22
  85.6 17.8 %all_to_all.21 = f32[128,8,128]{2,1,0:T(8,128)S(1)} all-to-all(f32[128,8,128]{2,1,0:T(8,128)S(1)} %reshape_reshape_reshape.22), channel_id=1, replica_groups=mesh['wide'=32,'narrow'=4] {'wide','narrow'}, dimensions={0} | all-to-all | bytes 1048576 | tf_op jit(solution)/shard_map/all_to_all | solution.py:44
  103.4 0.2 reshape_reshape_reshape.23
  103.6 1.8 %convolution_multiply_fusion = f32[8,64,256]{2,1,0:T(8,128)} fusion(f32[256,8,64]{2,1,0:T(8,128)S(1)} %reshape_reshape_reshape.23, s32[8,64,256]{2,1,0:T(8,128)S(1)} %copy-done, f32[256,256]{1,0:T(8,128)S(1)} %sine_add_fusion.2), kind=kOutput, calls=%fused_computation.2 | convolution fusion | flops 201850880 | bytes 1835008 | tf_op jit(solution)/shard_map/kxy,kz->xyz/dot_general | solution.py:69
  (9 shorter events, 0.1 us)
Async XLA Ops:
  3.9 25.1 %all-to-all-start = ((f32[128,8,128]{2,1,0:T(8,128)}), f32[128,8,128]{2,1,0:T(8,128)S(1)}, u32[]{:S(2)}, u32[]{:S(2)}) async-start(f32[128,8,128]{2,1,0:T(8,128)} %reshape_reshape_reshape.18), calls=%async_computation | async-start | bytes 1048576 | tf_op jit(solution)/shard_map/all_to_all | solution.py:44
  63.5 18.4 %all-to-all-start.2 = ((f32[128,8,128]{2,1,0:T(8,128)}), f32[128,8,128]{2,1,0:T(8,128)S(1)}, u32[]{:S(2)}, u32[]{:S(2)}) async-start(f32[128,8,128]{2,1,0:T(8,128)} %reshape_reshape_reshape.20), calls=%async_computation.2 | async-start | bytes 1048576 | tf_op jit(solution)/shard_map/all_to_all | solution.py:44
  85.6 18.0 %copy-start = (s32[8,64,256]{2,1,0:T(8,128)S(1)}, s32[8,64,256]{2,1,0:T(8,128)}, u32[]{:S(2)}) copy-start(s32[8,64,256]{2,1,0:T(8,128)} %param.3) | copy-start | bytes 1572868

commit v4 on v1

--- a/solution.py
+++ b/solution.py
@@ -1,6 +1,7 @@
 import math
 
 import jax
+import numpy as np
 import jax.numpy as jnp
 from jax import lax
 from jax.sharding import PartitionSpec as P
@@ -10,10 +11,9 @@
 
 
 def cas_table(length):
-    positions = jnp.arange(length, dtype=jnp.int32)
-    phase_steps = positions[:, None] * positions[None, :] % length
-    angles = phase_steps.astype(jnp.float32) * (2.0 * math.pi / length)
-    return jnp.cos(angles) + jnp.sin(angles)
+    positions = np.arange(length, dtype=np.int64)
+    angles = (positions[:, None] * positions[None, :] % length) * (2.0 * math.pi / length)
+    return jnp.asarray((np.cos(angles) + np.sin(angles)).astype(np.float32))
 
 
 def cas_columns(length, positions):

time: 114 us -> 104 us (0.912)
  matrix products: 19.9 us -> 9.34 us
    dot_general x2, matrix products: 3.83 us -> 1.19 us  [to_planes(): jnp.einsum('wqkxy,qyl->kwxl', arrived, cas.reshape(narrow, count_y, lengt...]
    dot_general x2, matrix products: 4.16 us -> 2.15 us  [to_planes(): along_z = jnp.einsum('xyz,zk->kxy', pencil, cas, precision=matmul_precision)]
    dot_general x2, matrix products: 3.36 us -> 1.37 us  [planes_forward(): return jnp.einsum('kxl,xm->kml', along_y, cas, precision=matmul_precision)]
  transfers between devices with their start and end apart: 2 -> 2, of which waited for: 2 -> 2; matrix products, arithmetic and copies ran while one was open for 3% -> 4% of each run, Pallas kernels for 0% -> 0%
where the time goes in v4:
time: 104 us
  blocking collectives  40.9 us (39%)
  waiting for transfers between devices  23.2 us (22%)
  starting transfers between devices  16.2 us (16%)
  matrix products  9.34 us (9%)
  local copies, waits for them, and re-layouts  8.56 us (8%)
  other arithmetic  5.12 us (5%)
    all_to_all x2, blocking collectives, exchange(): arrived = lax.all_to_all(flat.reshape(shape[0], tiles * 8, 128), ALL, 0, 0)  40.9 us
    all_to_all x2, waiting for transfers between devices, exchange(): arrived = lax.all_to_all(flat.reshape(shape[0], tiles * 8, 128), ALL, 0, 0)  23.2 us
    all_to_all x2, starting transfers between devices, exchange(): arrived = lax.all_to_all(flat.reshape(shape[0], tiles * 8, 128), ALL, 0, 0)  16.2 us
    add x2, other arithmetic, cas_columns(): return jnp.cos(angles) + jnp.sin(angles)  2.87 us
    another operation x3, local copies, waits for them, and re-layouts, exchange(): arrived = lax.all_to_all(flat.reshape(shape[0], tiles * 8, 128), ALL, 0, 0)  2.2 us
    dot_general x2, matrix products, to_planes(): along_z = jnp.einsum('xyz,zk->kxy', pencil, cas, precision=matmul_precision)  2.15 us
  transfers between devices with their start and end apart: 2, of which 2 were waited for; matrix products, arithmetic and copies ran while one was open for 4% of the time, Pallas kernels for 0%

profile of v4, /device:TPU:1, one launch (start us, length us, event | category | flops | bytes accessed | tf_op | source)
XLA Modules:
  0.0 103.7 jit_solution(11940659597011747055)
XLA Ops:
  0.0 1.5 %fusion.28 = f32[256,8,64]{0,2,1:T(8,128)S(1)} fusion(f32[256,256,1]{1,0,2:T(8,128)} %constant.101, s32[8,64,256]{2,1,0:T(8,128)} %param.3), kind=kOutput, calls=%fused_computation.53 | convolution fusion | flops 201457664 | bytes 1310720 | tf_op jit(solution)/shard_map/xyz,zk->kxy/dot_general | solution.py:53
  1.5 0.4 copy.14
  1.9 1.0 reshape_reshape_reshape.18
  2.9 11.5 %all-to-all-start = ((f32[128,8,128]{2,1,0:T(8,128)}), f32[128,8,128]{2,1,0:T(8,128)S(1)}, u32[]{:S(2)}, u32[]{:S(2)}) async-start(f32[128,8,128]{2,1,0:T(8,128)} %reshape_reshape_reshape.18), calls=%async_computation | async-start | bytes 1048576 | tf_op jit(solution)/shard_map/all_to_all | solution.py:44
  14.5 1.6 %sine_add_fusion = f32[256,32,12]{0,1,2:T(8,128)S(1)} fusion(s32[32,12]{0,1:T(8,128)S(1)} %add_select_fusion.3), kind=kLoop, calls=%fused_computation.64 | loop fusion | flops 1474560 | bytes 394752 | tf_op jit(solution)/shard_map/add | solution.py:23
  16.1 0.1 add_select_fusion.4
  16.2 1.2 %sine_add_fusion.1 = f32[256,4,72]{0,2,1:T(8,128)S(1)} fusion(s32[4,72]{1,0:T(4,128)S(1)} %add_select_fusion.4), kind=kLoop, calls=%fused_computation.72 | loop fusion | flops 1105920 | bytes 296064 | tf_op jit(solution)/shard_map/add | solution.py:23
  17.5 0.8 broadcast_add_fusion
  18.4 9.6 %all-to-all-done = f32[128,8,128]{2,1,0:T(8,128)S(1)} async-done(((f32[128,8,128]{2,1,0:T(8,128)}), f32[128,8,128]{2,1,0:T(8,128)S(1)}, u32[]{:S(2)}, u32[]{:S(2)}) %all-to-all-start) | async-done | bytes 524320 | tf_op jit(solution)/shard_map/all_to_all | solution.py:44
  28.0 0.2 reshape_reshape_reshape.19
  28.2 0.6 convolution_bitcast_fusion.3
  28.8 0.3 copy-done.3
  29.2 0.7 fusion.3
  29.8 0.5 convolution_bitcast_fusion.1
  30.3 0.8 convolution_bitcast_fusion
  31.2 0.9 copy.19
  32.1 1.1 %reshape.208 = f32[128,1728]{1,0:T(8,128)S(1)} reshape(f32[32,4,2,12,72]{4,3,2,1,0:T(8,128)S(1)} %copy.19) | data formatting | bytes 1769472 | tf_op jit(solution)/shard_map/reshape | solution.py:78
  33.2 0.1 pad_bitcast_fusion
  33.3 0.2 copy.38
  33.5 23.2 %all_to_all.20 = f32[128,16,128]{2,1,0:T(8,128)S(1)} all-to-all(f32[128,16,128]{2,1,0:T(8,128)S(1)} %bitcast.95), channel_id=1, replica_groups=mesh['wide'=32,'narrow'=4] {'wide','narrow'}, dimensions={0} | all-to-all | bytes 2097152 | tf_op jit(solution)/shard_map/all_to_all | solution.py:44
  56.7 0.3 copy.52
  57.0 0.1 slice.92
  57.1 0.2 reshape.211
  57.3 0.3 copy.20
  57.6 0.5 fusion.59
  58.1 0.3 fusion.55
  58.4 0.2 fusion.56
  58.6 0.8 negate_divide_fusion
  59.4 0.2 fusion.58
  59.6 0.1 fusion.57
  59.8 0.3 negate_divide_fusion.2
  60.1 0.6 fusion.15
  60.8 0.4 copy.21
  61.2 1.0 reshape_reshape_reshape.20
  62.2 4.7 %all-to-all-start.2 = ((f32[128,8,128]{2,1,0:T(8,128)}), f32[128,8,128]{2,1,0:T(8,128)S(1)}, u32[]{:S(2)}, u32[]{:S(2)}) async-start(f32[128,8,128]{2,1,0:T(8,128)} %reshape_reshape_reshape.20), calls=%async_computation.2 | async-start | bytes 1048576 | tf_op jit(solution)/shard_map/all_to_all | solution.py:44
  66.9 0.1 broadcast_and_fusion
  67.0 13.6 %all-to-all-done.2 = f32[128,8,128]{2,1,0:T(8,128)S(1)} async-done(((f32[128,8,128]{2,1,0:T(8,128)}), f32[128,8,128]{2,1,0:T(8,128)S(1)}, u32[]{:S(2)}, u32[]{:S(2)}) %all-to-all-start.2) | async-done | bytes 524320 | tf_op jit(solution)/shard_map/all_to_all | solution.py:44
  80.6 0.2 reshape_reshape_reshape.21
  80.8 0.6 convolution_bitcast_fusion.2
  81.4 0.7 fusion.6
  82.2 0.4 convolution_bitcast_fusion.4
  82.5 0.6 fusion.60
  83.2 0.5 reshape.213
  83.6 0.1 copy.53
  83.7 0.2 reshape_reshape_reshape.22
  83.9 17.8 %all_to_all.21 = f32[128,8,128]{2,1,0:T(8,128)S(1)} all-to-all(f32[128,8,128]{2,1,0:T(8,128)S(1)} %reshape_reshape_reshape.22), channel_id=1, replica_groups=mesh['wide'=32,'narrow'=4] {'wide','narrow'}, dimensions={0} | all-to-all | bytes 1048576 | tf_op jit(solution)/shard_map/all_to_all | solution.py:44
  101.7 0.2 reshape_reshape_reshape.23
  101.9 1.8 %convolution_multiply_fusion = f32[8,64,256]{2,1,0:T(8,128)} fusion(f32[256,256,1]{1,0,2:T(8,128)S(1)} %copy-done, f32[256,8,64]{2,1,0:T(8,128)S(1)} %reshape_reshape_reshape.23, s32[8,64,256]{2,1,0:T(8,128)S(1)} %copy-done.2), kind=kOutput, calls=%fused_computation.2 | convolution fusion | flops 201850880 | bytes 1835008 | tf_op jit(solution)/shard_map/kxy,kz->xyz/dot_general | solution.py:69
  (16 shorter events, 0.1 us)
Async XLA Ops:
  2.9 25.3 %copy-start.1 = (f32[4,64,256,1,1]{2,1,0,4,3:T(8,128)S(1)}, f32[4,64,256,1,1]{2,1,0,4,3:T(8,128)}, u32[]{:S(2)}) copy-start(f32[4,64,256,1,1]{2,1,0,4,3:T(8,128)} %constant.102) | copy-start | bytes 786436
  2.9 25.1 %all-to-all-start = ((f32[128,8,128]{2,1,0:T(8,128)}), f32[128,8,128]{2,1,0:T(8,128)S(1)}, u32[]{:S(2)}, u32[]{:S(2)}) async-start(f32[128,8,128]{2,1,0:T(8,128)} %reshape_reshape_reshape.18), calls=%async_computation | async-start | bytes 1048576 | tf_op jit(solution)/shard_map/all_to_all | solution.py:44
  18.3 10.5 %copy-start = (f32[256,256,1]{1,0,2:T(8,128)S(1)}, f32[256,256,1]{1,0,2:T(8,128)}, u32[]{:S(2)}) copy-start(f32[256,256,1]{1,0,2:T(8,128)} %constant.101) | copy-start | bytes 786436
  28.2 1.0 copy-start.3
  62.2 18.4 %all-to-all-start.2 = ((f32[128,8,128]{2,1,0:T(8,128)}), f32[128,8,128]{2,1,0:T(8,128)S(1)}, u32[]{:S(2)}, u32[]{:S(2)}) async-start(f32[128,8,128]{2,1,0:T(8,128)} %reshape_reshape_reshape.20), calls=%async_computation.2 | async-start | bytes 1048576 | tf_op jit(solution)/shard_map/all_to_all | solution.py:44
  67.0 14.4 %copy-start.4 = (f32[256,256]{0,1:T(8,128)S(1)}, f32[256,256]{0,1:T(8,128)}, u32[]{:S(2)}) copy-start(f32[256,256]{0,1:T(8,128)} %broadcast_add_fusion) | copy-start | bytes 786436
  83.9 18.0 %copy-start.2 = (s32[8,64,256]{2,1,0:T(8,128)S(1)}, s32[8,64,256]{2,1,0:T(8,128)}, u32[]{:S(2)}) copy-start(s32[8,64,256]{2,1,0:T(8,128)} %param.4) | copy-start | bytes 1572868

commit v5 on v4

--- a/solution.py
+++ b/solution.py
@@ -17,16 +17,15 @@
 
 
 def cas_columns(length, positions):
-    wavenumbers = jnp.arange(length, dtype=jnp.int32).reshape((length,) + (1,) * positions.ndim)
-    phase_steps = wavenumbers * positions[None] % length
-    angles = phase_steps.astype(jnp.float32) * (2.0 * math.pi / length)
-    return jnp.cos(angles) + jnp.sin(angles)
+    wavenumbers = np.arange(length, dtype=np.int64).reshape((length,) + (1,) * positions.ndim)
+    angles = (wavenumbers * positions[None] % length) * (2.0 * math.pi / length)
+    return jnp.asarray((np.cos(angles) + np.sin(angles)).astype(np.float32))
 
 
 def window_positions(length, count, width):
     blocks = length // count
-    starts = jnp.arange(blocks, dtype=jnp.int32)[:, None] * count - width
-    return (starts + jnp.arange(count + 2 * width, dtype=jnp.int32)[None, :]) % length
+    starts = np.arange(blocks, dtype=np.int64)[:, None] * count - width
+    return (starts + np.arange(count + 2 * width, dtype=np.int64)[None, :]) % length
 
 
 def eigen(wavenumber, length):
@@ -126,12 +125,8 @@
 
     heat_filter = 1.0 + heat_time * laplace
     laplace_safe = jnp.where(anchor, 1.0, laplace)
-    cas_x, cas_y = lax.optimization_barrier(
-        (
-            cas_columns(length, window_positions(length, count_x, 2)),
-            cas_columns(length, window_positions(length, count_y, 4)),
-        )
-    )
+    cas_x = cas_columns(length, window_positions(length, count_x, 2))
+    cas_y = cas_columns(length, window_positions(length, count_y, 4))
     source = sources.astype(jnp.float32)
     spectrum = planes_forward(to_planes(source, cas), cas)
     padded = to_pencil_with_halo(spectrum / heat_filter * scale, cas, cas_x, cas_y)

time: 104 us -> 104 us (level)
  waiting for transfers between devices: 23.2 us -> 26.9 us
  other arithmetic: 5.12 us -> 1.43 us
    all_to_all x2, waiting for transfers between devices: 23.2 us -> 26.9 us  [exchange(): arrived = lax.all_to_all(flat.reshape(shape[0], tiles * 8, 128), ALL, 0, 0)]
    add x2 -> x0, other arithmetic: 2.87 us -> none  [cas_columns(): return jnp.cos(angles) + jnp.sin(angles)]
  transfers between devices with their start and end apart: 2 -> 2, of which waited for: 2 -> 2; matrix products, arithmetic and copies ran while one was open for 4% -> 0% of each run, Pallas kernels for 0% -> 0%
where the time goes in v5:
time: 104 us
  blocking collectives  40.9 us (39%)
  waiting for transfers between devices  26.9 us (26%)
  starting transfers between devices  16.2 us (16%)
  matrix products  9.32 us (9%)
  local copies, waits for them, and re-layouts  8.57 us (8%)
  other arithmetic  1.43 us (1%)
    all_to_all x2, blocking collectives, exchange(): arrived = lax.all_to_all(flat.reshape(shape[0], tiles * 8, 128), ALL, 0, 0)  40.9 us
    all_to_all x2, waiting for transfers between devices, exchange(): arrived = lax.all_to_all(flat.reshape(shape[0], tiles * 8, 128), ALL, 0, 0)  26.9 us
    all_to_all x2, starting transfers between devices, exchange(): arrived = lax.all_to_all(flat.reshape(shape[0], tiles * 8, 128), ALL, 0, 0)  16.2 us
    another operation x3, local copies, waits for them, and re-layouts, exchange(): arrived = lax.all_to_all(flat.reshape(shape[0], tiles * 8, 128), ALL, 0, 0)  2.2 us
    dot_general x2, matrix products, to_planes(): along_z = jnp.einsum('xyz,zk->kxy', pencil, cas, precision=matmul_precision)  2.15 us
  transfers between devices with their start and end apart: 2, of which 2 were waited for; matrix products, arithmetic and copies ran while one was open for 0% of the time, Pallas kernels for 0%

profile of v5, /device:TPU:1, one launch (start us, length us, event | category | flops | bytes accessed | tf_op | source)
XLA Modules:
  0.0 103.7 jit_solution(1032749932180996492)
XLA Ops:
  0.0 1.5 %fusion.28 = f32[256,8,64]{0,2,1:T(8,128)S(1)} fusion(f32[256,256,1]{1,0,2:T(8,128)} %constant.57, s32[8,64,256]{2,1,0:T(8,128)} %param.5), kind=kOutput, calls=%fused_computation.50 | convolution fusion | flops 201457664 | bytes 1310720 | tf_op jit(solution)/shard_map/xyz,zk->kxy/dot_general | solution.py:52
  1.5 0.4 copy.16
  1.9 1.0 reshape_reshape_reshape.18
  2.9 11.5 %all-to-all-start = ((f32[128,8,128]{2,1,0:T(8,128)}), f32[128,8,128]{2,1,0:T(8,128)S(1)}, u32[]{:S(2)}, u32[]{:S(2)}) async-start(f32[128,8,128]{2,1,0:T(8,128)} %reshape_reshape_reshape.18), calls=%async_computation | async-start | bytes 1048576 | tf_op jit(solution)/shard_map/all_to_all | solution.py:43
  14.5 0.1 broadcast_add_fusion
  14.7 0.0 copy-start
  14.7 13.3 %all-to-all-done = f32[128,8,128]{2,1,0:T(8,128)S(1)} async-done(((f32[128,8,128]{2,1,0:T(8,128)}), f32[128,8,128]{2,1,0:T(8,128)S(1)}, u32[]{:S(2)}, u32[]{:S(2)}) %all-to-all-start) | async-done | bytes 524320 | tf_op jit(solution)/shard_map/all_to_all | solution.py:43
  28.0 0.2 reshape_reshape_reshape.19
  28.2 0.6 convolution_bitcast_fusion.3
  28.8 0.0 copy-start.3
  28.8 0.0 copy-start.4
  28.9 0.7 fusion.3
  29.5 0.3 copy-done.3
  29.8 0.5 convolution_bitcast_fusion.1
  30.4 0.8 convolution_bitcast_fusion
  31.2 0.9 copy.21
  32.1 1.1 %reshape.132 = f32[128,1728]{1,0:T(8,128)S(1)} reshape(f32[32,4,2,12,72]{4,3,2,1,0:T(8,128)S(1)} %copy.21) | data formatting | bytes 1769472 | tf_op jit(solution)/shard_map/reshape | solution.py:77
  33.2 0.1 pad_bitcast_fusion
  33.3 0.2 copy.41
  33.5 23.1 %all_to_all.20 = f32[128,16,128]{2,1,0:T(8,128)S(1)} all-to-all(f32[128,16,128]{2,1,0:T(8,128)S(1)} %bitcast.95), channel_id=1, replica_groups=mesh['wide'=32,'narrow'=4] {'wide','narrow'}, dimensions={0} | all-to-all | bytes 2097152 | tf_op jit(solution)/shard_map/all_to_all | solution.py:43
  56.7 0.3 copy.55
  57.0 0.1 slice.92
  57.1 0.2 reshape.135
  57.3 0.3 copy.22
  57.6 0.5 fusion.40
  58.1 0.3 fusion.36
  58.4 0.2 fusion.37
  58.6 0.8 negate_divide_fusion
  59.4 0.2 fusion.39
  59.6 0.1 fusion.38
  59.8 0.3 negate_divide_fusion.2
  60.1 0.6 fusion.15
  60.8 0.4 copy.23
  61.2 1.0 reshape_reshape_reshape.20
  62.2 4.7 %all-to-all-start.2 = ((f32[128,8,128]{2,1,0:T(8,128)}), f32[128,8,128]{2,1,0:T(8,128)S(1)}, u32[]{:S(2)}, u32[]{:S(2)}) async-start(f32[128,8,128]{2,1,0:T(8,128)} %reshape_reshape_reshape.20), calls=%async_computation.2 | async-start | bytes 1048576 | tf_op jit(solution)/shard_map/all_to_all | solution.py:43
  66.9 0.1 broadcast_and_fusion
  67.0 13.6 %all-to-all-done.2 = f32[128,8,128]{2,1,0:T(8,128)S(1)} async-done(((f32[128,8,128]{2,1,0:T(8,128)}), f32[128,8,128]{2,1,0:T(8,128)S(1)}, u32[]{:S(2)}, u32[]{:S(2)}) %all-to-all-start.2) | async-done | bytes 524320 | tf_op jit(solution)/shard_map/all_to_all | solution.py:43
  80.6 0.2 reshape_reshape_reshape.21
  80.8 0.6 convolution_bitcast_fusion.2
  81.4 0.7 fusion.6
  82.1 0.4 convolution_bitcast_fusion.4
  82.5 0.6 fusion.41
  83.2 0.5 reshape.137
  83.6 0.1 copy.56
  83.7 0.2 reshape_reshape_reshape.22
  83.9 17.8 %all_to_all.21 = f32[128,8,128]{2,1,0:T(8,128)S(1)} all-to-all(f32[128,8,128]{2,1,0:T(8,128)S(1)} %reshape_reshape_reshape.22), channel_id=1, replica_groups=mesh['wide'=32,'narrow'=4] {'wide','narrow'}, dimensions={0} | all-to-all | bytes 1048576 | tf_op jit(solution)/shard_map/all_to_all | solution.py:43
  101.7 0.2 reshape_reshape_reshape.23
  101.9 1.8 %convolution_multiply_fusion = f32[8,64,256]{2,1,0:T(8,128)} fusion(f32[256,256,1]{1,0,2:T(8,128)S(1)} %copy-done, f32[256,8,64]{2,1,0:T(8,128)S(1)} %reshape_reshape_reshape.23, s32[8,64,256]{2,1,0:T(8,128)S(1)} %copy-done.2), kind=kOutput, calls=%fused_computation.2 | convolution fusion | flops 201850880 | bytes 1835008 | tf_op jit(solution)/shard_map/kxy,kz->xyz/dot_general | solution.py:68
  (14 shorter events, 0.1 us)
Async XLA Ops:
  2.9 25.3 %copy-start.1 = (f32[4,64,256,1,1]{2,1,0,4,3:T(8,128)S(1)}, f32[4,64,256,1,1]{2,1,0,4,3:T(8,128)}, u32[]{:S(2)}) copy-start(f32[4,64,256,1,1]{2,1,0,4,3:T(8,128)} %constant.58) | copy-start | bytes 786436
  2.9 25.1 %all-to-all-start = ((f32[128,8,128]{2,1,0:T(8,128)}), f32[128,8,128]{2,1,0:T(8,128)S(1)}, u32[]{:S(2)}, u32[]{:S(2)}) async-start(f32[128,8,128]{2,1,0:T(8,128)} %reshape_reshape_reshape.18), calls=%async_computation | async-start | bytes 1048576 | tf_op jit(solution)/shard_map/all_to_all | solution.py:43
  14.6 14.2 %copy-start.5 = (f32[256,256]{0,1:T(8,128)}, f32[256,256]{0,1:T(8,128)S(1)}, u32[]{:S(2)}) copy-start(f32[256,256]{0,1:T(8,128)S(1)} %broadcast_add_fusion) | copy-start | bytes 786436
  14.7 14.2 %copy-start = (f32[256,256,1]{1,0,2:T(8,128)S(1)}, f32[256,256,1]{1,0,2:T(8,128)}, u32[]{:S(2)}) copy-start(f32[256,256,1]{1,0,2:T(8,128)} %constant.57) | copy-start | bytes 786436
  28.8 1.0 copy-start.3
  28.8 1.5 %copy-start.4 = (f32[256,4,72,1,1]{0,2,1,4,3:T(8,128)S(1)}, f32[256,4,72,1,1]{0,2,1,4,3:T(8,128)}, u32[]{:S(2)}) copy-start(f32[256,4,72,1,1]{0,2,1,4,3:T(8,128)} %constant.60) | copy-start | bytes 884740
  62.2 18.4 %all-to-all-start.2 = ((f32[128,8,128]{2,1,0:T(8,128)}), f32[128,8,128]{2,1,0:T(8,128)S(1)}, u32[]{:S(2)}, u32[]{:S(2)}) async-start(f32[128,8,128]{2,1,0:T(8,128)} %reshape_reshape_reshape.20), calls=%async_computation.2 | async-start | bytes 1048576 | tf_op jit(solution)/shard_map/all_to_all | solution.py:43
  67.0 14.4 %copy-start.6 = (f32[256,256]{0,1:T(8,128)S(1)}, f32[256,256]{0,1:T(8,128)}, u32[]{:S(2)}) copy-start(f32[256,256]{0,1:T(8,128)} %copy-done.5) | copy-start | bytes 786436
  83.9 18.0 %copy-start.2 = (s32[8,64,256]{2,1,0:T(8,128)S(1)}, s32[8,64,256]{2,1,0:T(8,128)}, u32[]{:S(2)}) copy-start(s32[8,64,256]{2,1,0:T(8,128)} %param.6) | copy-start | bytes 1572868
